TPU v7x, 256 devices: a whole 4x4x8 slice. The times are simulated.
256 devices in a mesh: tm: 32 (over y, z_hi, core), rows: 8 (over z_lo, x).
Axes of the slice: x: 4, y: 4, z: 8 (z_hi: 4, z_lo: 2; z = z_hi * 2 + z_lo), core: 2. Of those that a mesh axis runs over, the one named last changes fastest.
Arguments:
- latent: bfloat16 [32, 16, 128, 512], P('tm', 'rows'), may hold values from -32 to 32
- norm_gain: float32 [512], replicated, may hold values from 0.1 to 1.9
- conv_weight: bfloat16 [27, 512, 512], P(None, 'tm'), may hold values from -0.0546875 to 0.0546875
- grad_out: bfloat16 [32, 16, 128, 512], P('tm', 'rows'), may hold values from -6 to 6
Outputs:
- refined: bfloat16 [32, 16, 128, 512], P('tm', 'rows')
- grad_latent: float32 [32, 16, 128, 512], P('tm', 'rows')
All inputs are finite; a program needn't handle non-finite values.
Results may differ from a plain program's by a relative error of at most 0.0013.
The roundings to bfloat16 on the way count: a program that leaves them out, or rounds other values in their place, can miss the bound.
Values may be sent and summed in bfloat16 or wider, within the bound.
No kernel may reach another device: no remote copies, remote signals or barrier semaphores. Data moves between devices by JAX's collectives and lax.ppermute only.
A program may use at most 64 MiB of HBM per device.

v0:
```python
import jax
import jax.numpy as jnp
from jax import lax
from jax.sharding import PartitionSpec as P

GROUPS = 32
epsilon = 1e-06


def shifted(block, axis, distance):
    devices = range(lax.axis_size(axis))
    route = [(i - distance, i) for i in devices if i - distance in devices]
    return lax.ppermute(block, axis, route)


def with_halo(shard, sides, width):
    for axis, dim in sides:
        size, length = (lax.axis_size(axis), shard.shape[dim])
        up = [(i, (i + 1) % size) for i in range(size - 1)]
        down = [(j, i) for i, j in up]
        last = lax.slice_in_dim(shard, length - width, length, axis=dim)
        first = lax.slice_in_dim(shard, 0, width, axis=dim)
        before = lax.ppermute(last, axis, up)
        after = lax.ppermute(first, axis, down)
        shard = jnp.concatenate([before, shard, after], axis=dim)
    return shard


def grouped_view(values):
    return values.reshape(
        values.shape[0], values.shape[1] * values.shape[2], GROUPS, values.shape[3] // GROUPS
    )


def widen_columns(values):
    return jnp.pad(values, ((0, 0), (0, 0), (1, 1), (0, 0)))


def shards(latent, norm_gain, conv_weight, grad_out):
    frames_here, rows_here, columns, channels = latent.shape
    cell_count = lax.axis_size("rows") * rows_here * columns * (channels // GROUPS)
    full_weight = lax.all_gather(conv_weight, "tm", axis=1, tiled=True)
    latent_wide = latent.astype(jnp.float32)
    grouped = grouped_view(latent_wide)
    average = lax.psum(jnp.sum(grouped, axis=(1, 3)), "rows") / cell_count
    centred = grouped - average[:, None, :, None]
    spread = lax.psum(jnp.sum(centred * centred, axis=(1, 3)), "rows") / cell_count
    inverse = lax.rsqrt(spread + epsilon)
    normed_grouped = centred * inverse[:, None, :, None]
    normed = normed_grouped.reshape(latent.shape)
    scaled = normed * norm_gain
    sigmoid_value = jax.nn.sigmoid(scaled)
    activated = (scaled * sigmoid_value).astype(jnp.bfloat16)
    before_one = shifted(activated, "tm", 1)
    before_two = shifted(activated, "tm", 2)
    padded = with_halo(
        jnp.concatenate([before_two, before_one, activated], axis=0), (("rows", 1),), 1
    )
    after_one = shifted(grad_out, "tm", -1)
    after_two = shifted(grad_out, "tm", -2)
    padded_grad = with_halo(
        jnp.concatenate([grad_out, after_one, after_two], axis=0), (("rows", 1),), 1
    )
    padded = widen_columns(padded)
    padded_grad = widen_columns(padded_grad)
    conv_sum = jnp.zeros((frames_here * rows_here * columns, channels), jnp.float32)
    grad_act = jnp.zeros((frames_here * rows_here * columns, channels), jnp.float32)
    for time_tap in range(3):
        for row_tap in range(3):
            for col_tap in range(3):
                tap_weight = full_weight[time_tap * 9 + row_tap * 3 + col_tap]
                window = padded[
                    time_tap : time_tap + frames_here,
                    row_tap : row_tap + rows_here,
                    col_tap : col_tap + columns,
                ]
                conv_sum = conv_sum + jnp.dot(
                    window.reshape(-1, channels), tap_weight, preferred_element_type=jnp.float32
                )
                back_window = padded_grad[
                    2 - time_tap : 2 - time_tap + frames_here,
                    2 - row_tap : 2 - row_tap + rows_here,
                    2 - col_tap : 2 - col_tap + columns,
                ]
                grad_act = grad_act + lax.dot_general(
                    back_window.reshape(-1, channels),
                    tap_weight,
                    (((1,), (1,)), ((), ())),
                    preferred_element_type=jnp.float32,
                )
    refined = (latent_wide + conv_sum.reshape(latent.shape)).astype(jnp.bfloat16)
    grad_scaled = (
        grad_act.reshape(latent.shape) * sigmoid_value * (1.0 + scaled * (1.0 - sigmoid_value))
    )
    grad_normed = grouped_view(grad_scaled * norm_gain)
    first_sum, second_sum = lax.psum(
        (jnp.sum(grad_normed, axis=(1, 3)), jnp.sum(grad_normed * normed_grouped, axis=(1, 3))),
        "rows",
    )
    first = first_sum / cell_count
    second = second_sum / cell_count
    grad_norm_part = (
        grad_normed - first[:, None, :, None] - normed_grouped * second[:, None, :, None]
    ) * inverse[:, None, :, None]
    grad_latent = grad_out.astype(jnp.float32) + grad_norm_part.reshape(latent.shape)
    return (refined, grad_latent)


def solution(mesh):
    placed = (P("tm", "rows", None, None), P(), P(None, "tm", None), P("tm", "rows", None, None))
    return jax.shard_map(
        shards,
        mesh=mesh,
        in_specs=placed,
        out_specs=(P("tm", "rows", None, None), P("tm", "rows", None, None)),
        check_vma=False,
    )
```

profile of v0, /device:TPU:6, one launch (start us, length us, event | category | flops | bytes accessed | tf_op | source)
XLA Modules:
  0.0 219.8 jit_solution(12708673439425601817)
XLA Ops:
  7.2 0.7 all-gather.2.cloned.1.call-update
  7.9 1.3 collective-permute-start.4
  9.2 1.3 collective-permute-start.5
  10.5 1.0 convert_reduce_fusion
  11.7 16.1 %psum.28 = f32[1,32]{1,0:T(1,128)S(1)} all-reduce(f32[1,32]{1,0:T(1,128)S(1)} %bitcast.290), channel_id=1, replica_groups=mesh['tm'=32,'rows'=8] {'rows'}, use_global_device_ids=true, to_apply=%region_2.0 | all-reduce | flops 32 | bytes 256 | tf_op jit(solution)/shard_map/psum | solution.py:45
  27.8 1.0 constant_dynamic-update-slice_fusion.2
  28.8 5.3 %collective-permute-done.5 = bf16[1,2,128,512]{3,2,1,0:T(8,128)(2,1)S(1)} collective-permute-done((bf16[1,2,128,512]{3,2,1,0:T(8,128)(2,1)}, bf16[1,2,128,512]{3,2,1,0:T(8,128)(2,1)S(1)}, u32[]{:S(2)}, u32[]{:S(2)}) %collective-permute-start.5) | collective-permute-done | bytes 262176 | tf_op jit(solution)/shard_map/ppermute | solution.py:13
  34.3 0.6 copy-done.7
  34.9 1.9 collective-permute-start.6
  36.8 3.9 %collective-permute-start.7 = (bf16[3,1,128,512]{3,2,1,0:T(8,128)(2,1)S(1)}, bf16[3,1,128,512]{3,2,1,0:T(8,128)(2,1)S(1)}, u32[]{:S(2)}, u32[]{:S(2)}) collective-permute-start(bf16[3,1,128,512]{3,2,1,0:T(8,128)(2,1)S(1)} %get-tuple-element.59), channel_id=1, source_target_pairs={{1,0},{2,1},{3,2},{4,3},{5,4},{6,5},{7,6},{9,8},{10,9},{11,10},{12... | collective-permute-start | bytes 1179656 | tf_op jit(solution)/shard_map/ppermute | solution.py:24
  40.9 1.0 fusion.31
  42.1 22.3 %psum.29 = f32[1,32]{1,0:T(1,128)S(1)} all-reduce(f32[1,32]{1,0:T(1,128)S(1)} %bitcast.291), channel_id=1, replica_groups=mesh['tm'=32,'rows'=8] {'rows'}, use_global_device_ids=true, to_apply=%region_5.6 | all-reduce | flops 32 | bytes 256 | tf_op jit(solution)/shard_map/psum | solution.py:47
  64.6 1.2 pad_maximum_fusion.6
  65.8 0.4 select_maximum_fusion
  66.2 1.7 fusion.87
  67.9 52.9 %all-gather.2.cloned.1.call-done = bf16[27,512,512]{2,1,0:T(8,128)(2,1)} async-done(((bf16[27,16,512]{2,1,0:T(8,128)(2,1)}), bf16[27,512,512]{2,1,0:T(8,128)(2,1)}) %all-gather.2.cloned.1.call-update) | async-done | bytes 14155792 | tf_op jit(solution)/shard_map/all_gather | solution.py:42
  120.8 1.6 fusion.59
  122.4 2.1 fusion.41
  124.6 2.2 fusion.77
  126.7 1.4 fusion.53
  128.2 1.5 fusion.35
  129.7 1.5 fusion.71
  131.1 1.5 fusion.81
  132.6 1.4 fusion.65
  134.0 1.4 fusion.47
  135.5 1.5 fusion.79
  137.0 1.5 fusion.33
  138.4 1.3 fusion.75
  139.7 0.3 fusion.73
  140.1 0.3 fusion.69
  140.4 0.3 fusion.67
  140.7 0.3 fusion.63
  141.1 0.3 fusion.61
  141.4 0.3 fusion.57
  141.8 0.3 fusion.55
  142.1 0.3 fusion.51
  142.5 0.3 fusion.49
  142.8 0.3 fusion.45
  143.1 0.3 fusion.43
  143.5 0.3 fusion.39
  143.8 0.3 fusion.37
  144.1 0.3 fusion.83
  144.5 0.8 fusion.8
  145.3 0.3 fusion.85
  145.7 2.3 %collective-permute-start.1 = (bf16[1,2,128,512]{3,2,1,0:T(8,128)(2,1)S(1)}, bf16[1,2,128,512]{3,2,1,0:T(8,128)(2,1)S(1)}, u32[]{:S(2)}, u32[]{:S(2)}) collective-permute-start(bf16[1,2,128,512]{3,2,1,0:T(8,128)(2,1)S(1)} %get-tuple-element.62), channel_id=1, source_target_pairs={{0,8},{8,16},{16,24},{24,32},{32,40},{40,48},{48,56},{56,64},{64,7... | collective-permute-start | bytes 786440 | tf_op jit(solution)/shard_map/ppermute | solution.py:13
  148.0 6.9 %collective-permute-start = (bf16[1,2,128,512]{3,2,1,0:T(8,128)(2,1)S(1)}, bf16[1,2,128,512]{3,2,1,0:T(8,128)(2,1)S(1)}, u32[]{:S(2)}, u32[]{:S(2)}) collective-permute-start(bf16[1,2,128,512]{3,2,1,0:T(8,128)(2,1)S(1)} %get-tuple-element.62), channel_id=1, source_target_pairs={{0,16},{8,24},{16,32},{24,40},{32,48},{40,56},{48,64},{56,72},{64,... | collective-permute-start | bytes 786440 | tf_op jit(solution)/shard_map/ppermute | solution.py:13
  155.2 22.7 %all-reduce.2 = (f32[1,32]{1,0:T(1,128)S(1)}, f32[1,32]{1,0:T(1,128)S(1)}) all-reduce(f32[1,32]{1,0:T(1,128)S(1)} %bitcast.289, f32[1,32]{1,0:T(1,128)S(1)} %bitcast.288), channel_id=1, replica_groups=mesh['tm'=32,'rows'=8] {'rows'}, use_global_device_ids=true, to_apply=%region_11.12 | all-reduce | flops 64 | bytes 512 | tf_op jit(solution)/shard_map/psum | solution.py:96
  178.3 1.3 fusion.78
  179.8 3.7 %collective-permute-start.2 = (bf16[3,1,128,512]{3,2,1,0:T(8,128)(2,1)S(1)}, bf16[3,1,128,512]{3,2,1,0:T(8,128)(2,1)S(1)}, u32[]{:S(2)}, u32[]{:S(2)}) collective-permute-start(bf16[3,1,128,512]{3,2,1,0:T(8,128)(2,1)S(1)} %get-tuple-element.60), channel_id=1, source_target_pairs={{0,1},{1,2},{2,3},{3,4},{4,5},{5,6},{6,7},{8,9},{9,10},{10,11},{11... | collective-permute-start | bytes 1179656 | tf_op jit(solution)/shard_map/ppermute | solution.py:23
  183.6 2.3 %collective-permute-start.3 = (bf16[3,1,128,512]{3,2,1,0:T(8,128)(2,1)S(1)}, bf16[3,1,128,512]{3,2,1,0:T(8,128)(2,1)S(1)}, u32[]{:S(2)}, u32[]{:S(2)}) collective-permute-start(bf16[3,1,128,512]{3,2,1,0:T(8,128)(2,1)S(1)} %get-tuple-element.61), channel_id=1, source_target_pairs={{1,0},{2,1},{3,2},{4,3},{5,4},{6,5},{7,6},{9,8},{10,9},{11,10},{12... | collective-permute-start | bytes 1179656 | tf_op jit(solution)/shard_map/ppermute | solution.py:24
  185.9 1.5 fusion.42
  187.4 1.3 fusion.60
  188.7 4.1 %collective-permute-done.2 = bf16[3,1,128,512]{3,2,1,0:T(8,128)(2,1)S(1)} collective-permute-done((bf16[3,1,128,512]{3,2,1,0:T(8,128)(2,1)S(1)}, bf16[3,1,128,512]{3,2,1,0:T(8,128)(2,1)S(1)}, u32[]{:S(2)}, u32[]{:S(2)}) %collective-permute-start.2) | collective-permute-done | bytes 393248 | tf_op jit(solution)/shard_map/ppermute | solution.py:23
  192.9 5.6 %collective-permute-done.3 = bf16[3,1,128,512]{3,2,1,0:T(8,128)(2,1)S(1)} collective-permute-done((bf16[3,1,128,512]{3,2,1,0:T(8,128)(2,1)S(1)}, bf16[3,1,128,512]{3,2,1,0:T(8,128)(2,1)S(1)}, u32[]{:S(2)}, u32[]{:S(2)}) %collective-permute-start.3) | collective-permute-done | bytes 393248 | tf_op jit(solution)/shard_map/ppermute | solution.py:24
  198.4 0.7 select_maximum_fusion.2
  199.2 0.8 fusion.88
  200.1 1.8 fusion.66
  202.0 1.3 fusion.48
  203.3 1.3 fusion.82
  205.3 0.3 fusion.72
  206.8 0.3 fusion.70
  209.6 0.3 fusion.44
  210.8 1.1 fusion.11
  211.9 1.1 fusion.30
  (75 shorter events, 7.0 us)
Async XLA Ops:
  7.2 117.4 %copy-start.2 = (bf16[1,2,128,512]{3,2,1,0:T(8,128)(2,1)S(1)}, bf16[1,2,128,512]{3,2,1,0:T(8,128)(2,1)}, u32[]{:S(2)}) copy-start(bf16[1,2,128,512]{3,2,1,0:T(8,128)(2,1)} %param.7) | copy-start | bytes 786436
  7.2 113.7 %all-gather.2.cloned.1.call-start = ((), (), s32[]{:S(2)}) async-start(), calls=%async_computation | async-start | bytes 14598144 | tf_op jit(solution)/shard_map/all_gather | solution.py:42
  7.9 20.9 %collective-permute-start.4 = (bf16[1,2,128,512]{3,2,1,0:T(8,128)(2,1)}, bf16[1,2,128,512]{3,2,1,0:T(8,128)(2,1)S(1)}, u32[]{:S(2)}, u32[]{:S(2)}) collective-permute-start(bf16[1,2,128,512]{3,2,1,0:T(8,128)(2,1)} %param.7), channel_id=1, source_target_pairs={{8,0},{16,8},{24,16},{32,24},{40,32},{48,40},{56,48},{64,56},{72,6... | collective-permute-start | bytes 786440 | tf_op jit(solution)/shard_map/ppermute | solution.py:13
  9.2 24.9 %collective-permute-start.5 = (bf16[1,2,128,512]{3,2,1,0:T(8,128)(2,1)}, bf16[1,2,128,512]{3,2,1,0:T(8,128)(2,1)S(1)}, u32[]{:S(2)}, u32[]{:S(2)}) collective-permute-start(bf16[1,2,128,512]{3,2,1,0:T(8,128)(2,1)} %param.7), channel_id=1, source_target_pairs={{16,0},{24,8},{32,16},{40,24},{48,32},{56,40},{64,48},{72,56},{80,... | collective-permute-start | bytes 786440 | tf_op jit(solution)/shard_map/ppermute | solution.py:13
  28.8 5.5 %copy-start.6 = (bf16[1,2,128,512]{3,2,1,0:T(8,128)(2,1)}, bf16[1,2,128,512]{3,2,1,0:T(8,128)(2,1)S(1)}, u32[]{:S(2)}) copy-start(bf16[1,2,128,512]{3,2,1,0:T(8,128)(2,1)S(1)} %collective-permute-done.4) | copy-start | bytes 786436
  34.2 0.7 copy-start.7
  34.9 29.8 %collective-permute-start.6 = (bf16[3,1,128,512]{3,2,1,0:T(8,128)(2,1)S(1)}, bf16[3,1,128,512]{3,2,1,0:T(8,128)(2,1)S(1)}, u32[]{:S(2)}, u32[]{:S(2)}) collective-permute-start(bf16[3,1,128,512]{3,2,1,0:T(8,128)(2,1)S(1)} %get-tuple-element.58), channel_id=1, source_target_pairs={{0,1},{1,2},{2,3},{3,4},{4,5},{5,6},{6,7},{8,9},{9,10},{10,11},{11... | collective-permute-start | bytes 1179656 | tf_op jit(solution)/shard_map/ppermute | solution.py:23
  36.8 27.9 %collective-permute-start.7 = (bf16[3,1,128,512]{3,2,1,0:T(8,128)(2,1)S(1)}, bf16[3,1,128,512]{3,2,1,0:T(8,128)(2,1)S(1)}, u32[]{:S(2)}, u32[]{:S(2)}) collective-permute-start(bf16[3,1,128,512]{3,2,1,0:T(8,128)(2,1)S(1)} %get-tuple-element.59), channel_id=1, source_target_pairs={{1,0},{2,1},{3,2},{4,3},{5,4},{6,5},{7,6},{9,8},{10,9},{11,10},{12... | collective-permute-start | bytes 1179656 | tf_op jit(solution)/shard_map/ppermute | solution.py:24
  120.8 17.6 %copy-start = (bf16[27,512,512]{2,1,0:T(8,128)(2,1)S(1)}, bf16[27,512,512]{2,1,0:T(8,128)(2,1)}, u32[]{:S(2)}) copy-start(bf16[27,512,512]{2,1,0:T(8,128)(2,1)} %all-gather.2.cloned.1.call-done) | copy-start | bytes 42467332
  120.8 18.9 %copy-start.5 = (bf16[1,2,128,512]{3,2,1,0:T(8,128)(2,1)S(1)}, bf16[1,2,128,512]{3,2,1,0:T(8,128)(2,1)}, u32[]{:S(2)}) copy-start(bf16[1,2,128,512]{3,2,1,0:T(8,128)(2,1)} %get-tuple-element.11) | copy-start | bytes 786436
  120.8 19.2 %copy-start.4 = (bf16[1,2,128,512]{3,2,1,0:T(8,128)(2,1)S(1)}, bf16[1,2,128,512]{3,2,1,0:T(8,128)(2,1)}, u32[]{:S(2)}) copy-start(bf16[1,2,128,512]{3,2,1,0:T(8,128)(2,1)} %get-tuple-element.12) | copy-start | bytes 786436
  120.8 19.6 %copy-start.3 = (bf16[1,2,128,512]{3,2,1,0:T(8,128)(2,1)S(1)}, bf16[1,2,128,512]{3,2,1,0:T(8,128)(2,1)}, u32[]{:S(2)}) copy-start(bf16[1,2,128,512]{3,2,1,0:T(8,128)(2,1)} %get-tuple-element.13) | copy-start | bytes 786436
  141.1 4.2 %copy-start.1 = (bf16[1,2,128,512]{3,2,1,0:T(8,128)(2,1)S(1)}, bf16[1,2,128,512]{3,2,1,0:T(8,128)(2,1)}, u32[]{:S(2)}) copy-start(bf16[1,2,128,512]{3,2,1,0:T(8,128)(2,1)} %param.4) | copy-start | bytes 786436
  141.1 4.2 %copy-start.8 = (f32[512]{0:T(512)S(1)}, f32[512]{0:T(512)}, u32[]{:S(2)}) copy-start(f32[512]{0:T(512)} %param.5) | copy-start | bytes 6148
  145.3 59.3 %slice-start = ((s8[14155776]{0:T(1024)(128)(4,1)}), s8[1572864]{0:T(1024)(128)(4,1)S(1)}, s32[]{:S(2)}) async-start(s8[14155776]{0:T(1024)(128)(4,1)} %bitcast.231), calls=%async_computation.1 | async-start | bytes 3145728
  145.7 34.0 %collective-permute-start.1 = (bf16[1,2,128,512]{3,2,1,0:T(8,128)(2,1)S(1)}, bf16[1,2,128,512]{3,2,1,0:T(8,128)(2,1)S(1)}, u32[]{:S(2)}, u32[]{:S(2)}) collective-permute-start(bf16[1,2,128,512]{3,2,1,0:T(8,128)(2,1)S(1)} %get-tuple-element.62), channel_id=1, source_target_pairs={{0,8},{8,16},{16,24},{24,32},{32,40},{40,48},{48,56},{56,64},{64,7... | collective-permute-start | bytes 786440 | tf_op jit(solution)/shard_map/ppermute | solution.py:13
  148.0 31.7 %collective-permute-start = (bf16[1,2,128,512]{3,2,1,0:T(8,128)(2,1)S(1)}, bf16[1,2,128,512]{3,2,1,0:T(8,128)(2,1)S(1)}, u32[]{:S(2)}, u32[]{:S(2)}) collective-permute-start(bf16[1,2,128,512]{3,2,1,0:T(8,128)(2,1)S(1)} %get-tuple-element.62), channel_id=1, source_target_pairs={{0,16},{8,24},{16,32},{24,40},{32,48},{40,56},{48,64},{56,72},{64,... | collective-permute-start | bytes 786440 | tf_op jit(solution)/shard_map/ppermute | solution.py:13
  179.8 13.0 %collective-permute-start.2 = (bf16[3,1,128,512]{3,2,1,0:T(8,128)(2,1)S(1)}, bf16[3,1,128,512]{3,2,1,0:T(8,128)(2,1)S(1)}, u32[]{:S(2)}, u32[]{:S(2)}) collective-permute-start(bf16[3,1,128,512]{3,2,1,0:T(8,128)(2,1)S(1)} %get-tuple-element.60), channel_id=1, source_target_pairs={{0,1},{1,2},{2,3},{3,4},{4,5},{5,6},{6,7},{8,9},{9,10},{10,11},{11... | collective-permute-start | bytes 1179656 | tf_op jit(solution)/shard_map/ppermute | solution.py:23
  183.6 14.8 %collective-permute-start.3 = (bf16[3,1,128,512]{3,2,1,0:T(8,128)(2,1)S(1)}, bf16[3,1,128,512]{3,2,1,0:T(8,128)(2,1)S(1)}, u32[]{:S(2)}, u32[]{:S(2)}) collective-permute-start(bf16[3,1,128,512]{3,2,1,0:T(8,128)(2,1)S(1)} %get-tuple-element.61), channel_id=1, source_target_pairs={{1,0},{2,1},{3,2},{4,3},{5,4},{6,5},{7,6},{9,8},{10,9},{11,10},{12... | collective-permute-start | bytes 1179656 | tf_op jit(solution)/shard_map/ppermute | solution.py:24
  185.9 18.8 %slice-start.1 = ((s8[14155776]{0:T(1024)(128)(4,1)}), s8[4194304]{0:T(1024)(128)(4,1)S(1)}, s32[]{:S(2)}) async-start(s8[14155776]{0:T(1024)(128)(4,1)} %bitcast.231), calls=%async_computation.2 | async-start | bytes 8388608
  199.2 5.5 %slice-start.2 = ((s8[14155776]{0:T(1024)(128)(4,1)}), s8[4194304]{0:T(1024)(128)(4,1)S(1)}, s32[]{:S(2)}) async-start(s8[14155776]{0:T(1024)(128)(4,1)} %bitcast.231), calls=%async_computation.3 | async-start | bytes 8388608
  199.9 4.7 %slice-start.3 = ((s8[14155776]{0:T(1024)(128)(4,1)}), s8[4194304]{0:T(1024)(128)(4,1)S(1)}, s32[]{:S(2)}) async-start(s8[14155776]{0:T(1024)(128)(4,1)} %bitcast.231), calls=%async_computation.4 | async-start | bytes 8388608
Sparse Core Ops, SparseCore 0:
  10.6 110.1 all-gather.1
where the time goes:
time: 221 us; the launch traced here: 220 us
  waiting for transfers between devices  68.6 us (31%)
  blocking collectives  61.2 us (28%)
  matrix products  39.8 us (18%)
  starting transfers between devices  23.6 us (11%)
  between operations  14.8 us (7%)
  other arithmetic  6.57 us (3%)
  local copies, waits for them, and re-layouts  5.16 us (2%)
    all_gather x1, waiting for transfers between devices, shards(): full_weight = lax.all_gather(conv_weight, 'tm', axis=1, tiled=True)  52.9 us
    dot_general x27, matrix products, shards(): lax.dot_general(back_window.reshape(-1, channels), tap_weight, (((1,), (1...  24.2 us
    psum x1, blocking collectives, shards(): lax.psum((jnp.sum(grad_normed, axis=(1, 3)), jnp.sum(grad_normed * normed...  22.7 us
    psum x1, blocking collectives, shards(): lax.psum(jnp.sum(centred * centred, axis=(1, 3)), 'rows') / cell_count  22.3 us
    psum x1, blocking collectives, shards(): average = lax.psum(jnp.sum(grouped, axis=(1, 3)), 'rows') / cell_count  16.1 us
    dot_general x27, matrix products, shards(): jnp.dot(window.reshape(-1, channels), tap_weight, preferred_element_type=...  15.7 us
    ppermute x4, starting transfers between devices, shifted(): return lax.ppermute(block, axis, route)  11.8 us
    ppermute x2, starting transfers between devices, with_halo(): after = lax.ppermute(first, axis, down)  6.21 us
  transfers between devices with their start and end apart: 9, of which 4 were waited for; matrix products, arithmetic and copies ran while one was open for 5% of the time, Pallas kernels for 0%

commit v1 on v0

--- a/solution.py
+++ b/solution.py
@@ -39,7 +39,9 @@
 def shards(latent, norm_gain, conv_weight, grad_out):
     frames_here, rows_here, columns, channels = latent.shape
     cell_count = lax.axis_size("rows") * rows_here * columns * (channels // GROUPS)
-    full_weight = lax.all_gather(conv_weight, "tm", axis=1, tiled=True)
+    full_weight = jnp.concatenate(
+        lax.all_to_all(jnp.stack([conv_weight] * lax.axis_size("tm")), "tm", 0, 0), axis=1
+    )
     latent_wide = latent.astype(jnp.float32)
     grouped = grouped_view(latent_wide)
     average = lax.psum(jnp.sum(grouped, axis=(1, 3)), "rows") / cell_count

time: 221 us -> 466 us (2.11)
  the two profiles are of different devices: /device:TPU:6 before, /device:TPU:22 now
where the time goes in v1:
time: 466 us; the launch traced here: 465 us
  blocking collectives  363 us (78%)
  starting transfers between devices  41.8 us (9%)
  local copies, waits for them, and re-layouts  21.6 us (5%)
  matrix products  19.4 us (4%)
  waiting for transfers between devices  11.6 us (2%)
  other arithmetic  5.54 us (1%)
    psum x1, blocking collectives, shards(): average = lax.psum(jnp.sum(grouped, axis=(1, 3)), 'rows') / cell_count  322 us
    psum x1, blocking collectives, shards(): lax.psum((jnp.sum(grad_normed, axis=(1, 3)), jnp.sum(grad_normed * normed...  23 us
    psum x1, blocking collectives, shards(): lax.psum(jnp.sum(centred * centred, axis=(1, 3)), 'rows') / cell_count  18.2 us
    ppermute x4, starting transfers between devices, shifted(): return lax.ppermute(block, axis, route)  15.9 us
    all_to_all x1, starting transfers between devices, shards(): lax.all_to_all(jnp.stack([conv_weight] * lax.axis_size('tm')), 'tm', 0, 0)  11.8 us
    ppermute x2, waiting for transfers between devices, with_halo(): after = lax.ppermute(first, axis, down)  11.6 us
    ppermute x2, starting transfers between devices, with_halo(): before = lax.ppermute(last, axis, up)  10 us
    dot_general x27, matrix products, shards(): jnp.dot(window.reshape(-1, channels), tap_weight, preferred_element_type=...  9.86 us
  transfers between devices with their start and end apart: 9, of which 1 were waited for; matrix products, arithmetic and copies ran while one was open for 2% of the time, Pallas kernels for 0%

profile of v1, /device:TPU:22, one launch (start us, length us, event | category | flops | bytes accessed | tf_op | source)
XLA Modules:
  0.0 465.0 jit_solution(12013309357543813674)
XLA Ops:
  0.6 7.9 %stack.2 = bf16[32,27,16,512]{3,2,1,0:T(8,128)(2,1)} broadcast(bf16[27,16,512]{2,1,0:T(8,128)(2,1)} %param.6), dimensions={1,2,3} | broadcast | bytes 14598144 | tf_op jit(solution)/shard_map/stack | solution.py:43
  8.5 11.8 %all-to-all-start = ((bf16[32,27,16,512]{3,2,1,0:T(8,128)(2,1)}), bf16[32,27,16,512]{3,2,1,0:T(8,128)(2,1)}, u32[]{:S(2)}, u32[]{:S(2)}) async-start(bf16[32,27,16,512]{3,2,1,0:T(8,128)(2,1)} %stack.2), calls=%async_computation | async-start | bytes 28311552 | tf_op jit(solution)/shard_map/all_to_all | solution.py:43
  20.3 5.2 %collective-permute-start.4 = (bf16[1,2,128,512]{3,2,1,0:T(8,128)(2,1)S(1)}, bf16[1,2,128,512]{3,2,1,0:T(8,128)(2,1)S(1)}, u32[]{:S(2)}, u32[]{:S(2)}) collective-permute-start(bf16[1,2,128,512]{3,2,1,0:T(8,128)(2,1)S(1)} %copy-done.45), channel_id=1, source_target_pairs={{8,0},{16,8},{24,16},{32,24},{40,32},{48,40},{56,48},{64,56},{72,6... | collective-permute-start | bytes 786440 | tf_op jit(solution)/shard_map/ppermute | solution.py:13
  25.5 4.3 collective-permute-start.5
  30.0 321.6 %psum.28 = f32[1,32]{1,0:T(1,128)S(1)} all-reduce(f32[1,32]{1,0:T(1,128)S(1)} %bitcast.316), channel_id=1, replica_groups=mesh['tm'=32,'rows'=8] {'rows'}, use_global_device_ids=true, to_apply=%region_2.0 | all-reduce | flops 32 | bytes 256 | tf_op jit(solution)/shard_map/psum | solution.py:47
  351.8 0.5 copy-done.71
  352.4 6.0 %collective-permute-start.6 = (bf16[3,1,128,512]{3,2,1,0:T(8,128)(2,1)S(1)}, bf16[3,1,128,512]{3,2,1,0:T(8,128)(2,1)S(1)}, u32[]{:S(2)}, u32[]{:S(2)}) collective-permute-start(bf16[3,1,128,512]{3,2,1,0:T(8,128)(2,1)S(1)} %get-tuple-element.85), channel_id=1, source_target_pairs={{0,1},{1,2},{2,3},{3,4},{4,5},{5,6},{6,7},{8,9},{9,10},{10,11},{11... | collective-permute-start | bytes 1179656 | tf_op jit(solution)/shard_map/ppermute | solution.py:23
  358.4 1.9 collective-permute-start.7
  360.8 18.2 %psum.29 = f32[1,32]{1,0:T(1,128)S(1)} all-reduce(f32[1,32]{1,0:T(1,128)S(1)} %bitcast.317), channel_id=1, replica_groups=mesh['tm'=32,'rows'=8] {'rows'}, use_global_device_ids=true, to_apply=%region_5.6 | all-reduce | flops 32 | bytes 256 | tf_op jit(solution)/shard_map/psum | solution.py:49
  379.1 1.2 pad_maximum_fusion.6
  380.4 0.4 select_maximum_fusion
  380.8 2.1 fusion.37
  383.0 2.6 fusion.36
  385.7 5.8 %fusion.35 = (bf16[1,32,16,512]{3,2,0,1:T(8,128)(2,1)S(1)}, bf16[1,32,16,512]{3,2,0,1:T(8,128)(2,1)S(1)}, bf16[1,32,16,512]{3,2,0,1:T(8,128)(2,1)S(1)}, bf16[1,3...) fusion(bf16[27,32,16,512]{3,2,0,1:T(8,128)(2,1)} %bitcast.5), kind=kLoop, calls=%fused_computation.69 | loop fusion | bytes 19922944 | tf_op jit(solution)/shard_map/slice | solution.py:73
  391.7 0.3 fusion.75
  392.1 0.3 fusion.67
  392.5 0.3 fusion.74
  392.8 0.3 fusion.73
  393.2 0.3 fusion.72
  393.6 0.3 fusion.71
  393.9 0.3 fusion.70
  394.3 0.3 fusion.69
  394.7 0.3 fusion.92
  395.0 0.3 fusion.68
  395.4 0.3 fusion.91
  395.7 0.3 fusion.90
  396.1 0.3 fusion.88
  396.5 0.3 fusion.87
  396.8 0.3 fusion.86
  397.2 0.3 fusion.85
  397.6 0.3 fusion.84
  397.9 0.3 fusion.83
  398.3 0.3 fusion.82
  398.6 0.3 fusion.81
  399.0 0.3 fusion.80
  399.4 0.3 fusion.79
  399.7 0.3 fusion.78
  400.1 0.3 fusion.77
  400.4 0.3 fusion.76
  400.8 0.3 fusion.89
  401.1 1.0 fusion.8
  402.1 1.1 fusion.33
  403.3 1.9 collective-permute-start.1
  405.2 4.5 collective-permute-start
  410.1 23.0 %all-reduce.2 = (f32[1,32]{1,0:T(1,128)S(1)}, f32[1,32]{1,0:T(1,128)S(1)}) all-reduce(f32[1,32]{1,0:T(1,128)S(1)} %bitcast.315, f32[1,32]{1,0:T(1,128)S(1)} %bitcast.314), channel_id=1, replica_groups=mesh['tm'=32,'rows'=8] {'rows'}, use_global_device_ids=true, to_apply=%region_11.12 | all-reduce | flops 64 | bytes 512 | tf_op jit(solution)/shard_map/psum | solution.py:98
  433.4 1.4 fusion.63
  435.1 4.1 collective-permute-start.2
  439.2 2.1 collective-permute-start.3
  441.3 0.3 fusion.54
  441.6 0.3 fusion.45
  441.9 11.6 %collective-permute-done.3 = bf16[3,1,128,512]{3,2,1,0:T(8,128)(2,1)S(1)} collective-permute-done((bf16[3,1,128,512]{3,2,1,0:T(8,128)(2,1)S(1)}, bf16[3,1,128,512]{3,2,1,0:T(8,128)(2,1)S(1)}, u32[]{:S(2)}, u32[]{:S(2)}) %collective-permute-start.3) | collective-permute-done | bytes 393248 | tf_op jit(solution)/shard_map/ppermute | solution.py:24
  453.6 0.3 fusion.65
  454.0 0.3 fusion.48
  454.3 0.3 fusion.57
  455.6 0.7 select_maximum_fusion.2
  456.4 0.8 fusion.38
  459.7 0.3 fusion.52
  461.2 0.3 fusion.59
  461.5 0.3 fusion.61
  461.8 0.3 fusion.62
  462.1 0.3 fusion.41
  462.4 0.3 fusion.64
  462.8 1.1 fusion.11
  464.0 1.1 fusion.30
  (202 shorter events, 6.9 us)
Async XLA Ops:
  8.5 11.8 %copy-start.45 = (bf16[1,2,128,512]{3,2,1,0:T(8,128)(2,1)S(1)}, bf16[1,2,128,512]{3,2,1,0:T(8,128)(2,1)}, u32[]{:S(2)}) copy-start(bf16[1,2,128,512]{3,2,1,0:T(8,128)(2,1)} %param.7) | copy-start | bytes 786436
  8.5 21.3 %copy-start.43 = (bf16[1,2,128,512]{3,2,1,0:T(8,128)(2,1)S(1)}, bf16[1,2,128,512]{3,2,1,0:T(8,128)(2,1)}, u32[]{:S(2)}) copy-start(bf16[1,2,128,512]{3,2,1,0:T(8,128)(2,1)} %param.4) | copy-start | bytes 786436
  8.5 374.5 %all-to-all-start = ((bf16[32,27,16,512]{3,2,1,0:T(8,128)(2,1)}), bf16[32,27,16,512]{3,2,1,0:T(8,128)(2,1)}, u32[]{:S(2)}, u32[]{:S(2)}) async-start(bf16[32,27,16,512]{3,2,1,0:T(8,128)(2,1)} %stack.2), calls=%async_computation | async-start | bytes 28311552 | tf_op jit(solution)/shard_map/all_to_all | solution.py:43
  20.3 331.4 %collective-permute-start.4 = (bf16[1,2,128,512]{3,2,1,0:T(8,128)(2,1)S(1)}, bf16[1,2,128,512]{3,2,1,0:T(8,128)(2,1)S(1)}, u32[]{:S(2)}, u32[]{:S(2)}) collective-permute-start(bf16[1,2,128,512]{3,2,1,0:T(8,128)(2,1)S(1)} %copy-done.45), channel_id=1, source_target_pairs={{8,0},{16,8},{24,16},{32,24},{40,32},{48,40},{56,48},{64,56},{72,6... | collective-permute-start | bytes 786440 | tf_op jit(solution)/shard_map/ppermute | solution.py:13
  25.5 326.2 %collective-permute-start.5 = (bf16[1,2,128,512]{3,2,1,0:T(8,128)(2,1)S(1)}, bf16[1,2,128,512]{3,2,1,0:T(8,128)(2,1)S(1)}, u32[]{:S(2)}, u32[]{:S(2)}) collective-permute-start(bf16[1,2,128,512]{3,2,1,0:T(8,128)(2,1)S(1)} %copy-done.45), channel_id=1, source_target_pairs={{16,0},{24,8},{32,16},{40,24},{48,32},{56,40},{64,48},{72,56},{80,... | collective-permute-start | bytes 786440 | tf_op jit(solution)/shard_map/ppermute | solution.py:13
  352.4 26.7 %collective-permute-start.6 = (bf16[3,1,128,512]{3,2,1,0:T(8,128)(2,1)S(1)}, bf16[3,1,128,512]{3,2,1,0:T(8,128)(2,1)S(1)}, u32[]{:S(2)}, u32[]{:S(2)}) collective-permute-start(bf16[3,1,128,512]{3,2,1,0:T(8,128)(2,1)S(1)} %get-tuple-element.85), channel_id=1, source_target_pairs={{0,1},{1,2},{2,3},{3,4},{4,5},{5,6},{6,7},{8,9},{9,10},{10,11},{11... | collective-permute-start | bytes 1179656 | tf_op jit(solution)/shard_map/ppermute | solution.py:23
  358.4 20.7 %collective-permute-start.7 = (bf16[3,1,128,512]{3,2,1,0:T(8,128)(2,1)S(1)}, bf16[3,1,128,512]{3,2,1,0:T(8,128)(2,1)S(1)}, u32[]{:S(2)}, u32[]{:S(2)}) collective-permute-start(bf16[3,1,128,512]{3,2,1,0:T(8,128)(2,1)S(1)} %get-tuple-element.86), channel_id=1, source_target_pairs={{1,0},{2,1},{3,2},{4,3},{5,4},{6,5},{7,6},{9,8},{10,9},{11,10},{12... | collective-permute-start | bytes 1179656 | tf_op jit(solution)/shard_map/ppermute | solution.py:24
  385.6 6.1 %copy-start.4 = (bf16[1,32,16,512]{3,2,0,1:T(8,128)(2,1)}, bf16[1,32,16,512]{3,2,0,1:T(8,128)(2,1)S(1)}, u32[]{:S(2)}) copy-start(bf16[1,32,16,512]{3,2,0,1:T(8,128)(2,1)S(1)} %get-tuple-element.27) | copy-start | bytes 1572868
  385.6 6.8 %copy-start.32 = (bf16[1,32,16,512]{3,2,0,1:T(8,128)(2,1)}, bf16[1,32,16,512]{3,2,0,1:T(8,128)(2,1)S(1)}, u32[]{:S(2)}) copy-start(bf16[1,32,16,512]{3,2,0,1:T(8,128)(2,1)S(1)} %get-tuple-element.28) | copy-start | bytes 1572868
  385.6 7.2 %copy-start.8 = (bf16[1,32,16,512]{3,2,0,1:T(8,128)(2,1)}, bf16[1,32,16,512]{3,2,0,1:T(8,128)(2,1)S(1)}, u32[]{:S(2)}) copy-start(bf16[1,32,16,512]{3,2,0,1:T(8,128)(2,1)S(1)} %get-tuple-element.29) | copy-start | bytes 1572868
  385.7 7.5 %copy-start.12 = (bf16[1,32,16,512]{3,2,0,1:T(8,128)(2,1)}, bf16[1,32,16,512]{3,2,0,1:T(8,128)(2,1)S(1)}, u32[]{:S(2)}) copy-start(bf16[1,32,16,512]{3,2,0,1:T(8,128)(2,1)S(1)} %get-tuple-element.30) | copy-start | bytes 1572868
  385.7 7.9 %copy-start.36 = (bf16[1,32,16,512]{3,2,0,1:T(8,128)(2,1)}, bf16[1,32,16,512]{3,2,0,1:T(8,128)(2,1)S(1)}, u32[]{:S(2)}) copy-start(bf16[1,32,16,512]{3,2,0,1:T(8,128)(2,1)S(1)} %get-tuple-element.31) | copy-start | bytes 1572868
  385.7 8.2 %copy-start.16 = (bf16[1,32,16,512]{3,2,0,1:T(8,128)(2,1)}, bf16[1,32,16,512]{3,2,0,1:T(8,128)(2,1)S(1)}, u32[]{:S(2)}) copy-start(bf16[1,32,16,512]{3,2,0,1:T(8,128)(2,1)S(1)} %get-tuple-element.32) | copy-start | bytes 1572868
  385.7 8.6 %copy-start.20 = (bf16[1,32,16,512]{3,2,0,1:T(8,128)(2,1)}, bf16[1,32,16,512]{3,2,0,1:T(8,128)(2,1)S(1)}, u32[]{:S(2)}) copy-start(bf16[1,32,16,512]{3,2,0,1:T(8,128)(2,1)S(1)} %get-tuple-element.33) | copy-start | bytes 1572868
  385.7 6.0 %copy-start.70 = (bf16[1,2,128,512]{3,2,1,0:T(8,128)(2,1)S(1)}, bf16[1,2,128,512]{3,2,1,0:T(8,128)(2,1)}, u32[]{:S(2)}) copy-start(bf16[1,2,128,512]{3,2,1,0:T(8,128)(2,1)} %get-tuple-element.46) | copy-start | bytes 786436
  385.7 6.4 %copy-start.69 = (bf16[1,2,128,512]{3,2,1,0:T(8,128)(2,1)S(1)}, bf16[1,2,128,512]{3,2,1,0:T(8,128)(2,1)}, u32[]{:S(2)}) copy-start(bf16[1,2,128,512]{3,2,1,0:T(8,128)(2,1)} %get-tuple-element.34) | copy-start | bytes 786436
  385.7 6.7 %copy-start.63 = (bf16[1,2,128,512]{3,2,1,0:T(8,128)(2,1)S(1)}, bf16[1,2,128,512]{3,2,1,0:T(8,128)(2,1)}, u32[]{:S(2)}) copy-start(bf16[1,2,128,512]{3,2,1,0:T(8,128)(2,1)} %get-tuple-element.84) | copy-start | bytes 786436
  391.5 3.1 copy-start.24
  391.5 3.5 copy-start.28
  391.6 3.8 copy-start.38
  391.6 5.2 %copy-start.30 = (bf16[1,32,16,512]{3,2,0,1:T(8,128)(2,1)}, bf16[1,32,16,512]{3,2,0,1:T(8,128)(2,1)S(1)}, u32[]{:S(2)}) copy-start(bf16[1,32,16,512]{3,2,0,1:T(8,128)(2,1)S(1)} %get-tuple-element.15) | copy-start | bytes 1572868
  391.6 5.6 %copy-start = (bf16[1,32,16,512]{3,2,0,1:T(8,128)(2,1)}, bf16[1,32,16,512]{3,2,0,1:T(8,128)(2,1)S(1)}, u32[]{:S(2)}) copy-start(bf16[1,32,16,512]{3,2,0,1:T(8,128)(2,1)S(1)} %get-tuple-element.16) | copy-start | bytes 1572868
  391.6 5.9 %copy-start.2 = (bf16[1,32,16,512]{3,2,0,1:T(8,128)(2,1)}, bf16[1,32,16,512]{3,2,0,1:T(8,128)(2,1)S(1)}, u32[]{:S(2)}) copy-start(bf16[1,32,16,512]{3,2,0,1:T(8,128)(2,1)S(1)} %get-tuple-element.17) | copy-start | bytes 1572868
  391.6 6.3 %copy-start.34 = (bf16[1,32,16,512]{3,2,0,1:T(8,128)(2,1)}, bf16[1,32,16,512]{3,2,0,1:T(8,128)(2,1)S(1)}, u32[]{:S(2)}) copy-start(bf16[1,32,16,512]{3,2,0,1:T(8,128)(2,1)S(1)} %get-tuple-element.18) | copy-start | bytes 1572868
  391.6 6.7 %copy-start.6 = (bf16[1,32,16,512]{3,2,0,1:T(8,128)(2,1)}, bf16[1,32,16,512]{3,2,0,1:T(8,128)(2,1)S(1)}, u32[]{:S(2)}) copy-start(bf16[1,32,16,512]{3,2,0,1:T(8,128)(2,1)S(1)} %get-tuple-element.19) | copy-start | bytes 1572868
  391.6 7.0 %copy-start.10 = (bf16[1,32,16,512]{3,2,0,1:T(8,128)(2,1)}, bf16[1,32,16,512]{3,2,0,1:T(8,128)(2,1)S(1)}, u32[]{:S(2)}) copy-start(bf16[1,32,16,512]{3,2,0,1:T(8,128)(2,1)S(1)} %get-tuple-element.20) | copy-start | bytes 1572868
  391.6 7.4 %copy-start.40 = (bf16[1,32,16,512]{3,2,0,1:T(8,128)(2,1)}, bf16[1,32,16,512]{3,2,0,1:T(8,128)(2,1)S(1)}, u32[]{:S(2)}) copy-start(bf16[1,32,16,512]{3,2,0,1:T(8,128)(2,1)S(1)} %get-tuple-element.21) | copy-start | bytes 1572868
  391.6 7.7 %copy-start.14 = (bf16[1,32,16,512]{3,2,0,1:T(8,128)(2,1)}, bf16[1,32,16,512]{3,2,0,1:T(8,128)(2,1)S(1)}, u32[]{:S(2)}) copy-start(bf16[1,32,16,512]{3,2,0,1:T(8,128)(2,1)S(1)} %get-tuple-element.22) | copy-start | bytes 1572868
  391.6 8.0 %copy-start.18 = (bf16[1,32,16,512]{3,2,0,1:T(8,128)(2,1)}, bf16[1,32,16,512]{3,2,0,1:T(8,128)(2,1)S(1)}, u32[]{:S(2)}) copy-start(bf16[1,32,16,512]{3,2,0,1:T(8,128)(2,1)S(1)} %get-tuple-element.23) | copy-start | bytes 1572868
  391.7 8.4 %copy-start.26 = (bf16[1,32,16,512]{3,2,0,1:T(8,128)(2,1)}, bf16[1,32,16,512]{3,2,0,1:T(8,128)(2,1)S(1)}, u32[]{:S(2)}) copy-start(bf16[1,32,16,512]{3,2,0,1:T(8,128)(2,1)S(1)} %get-tuple-element.24) | copy-start | bytes 1572868
  391.7 8.7 %copy-start.22 = (bf16[1,32,16,512]{3,2,0,1:T(8,128)(2,1)}, bf16[1,32,16,512]{3,2,0,1:T(8,128)(2,1)S(1)}, u32[]{:S(2)}) copy-start(bf16[1,32,16,512]{3,2,0,1:T(8,128)(2,1)S(1)} %get-tuple-element.25) | copy-start | bytes 1572868
  391.7 9.1 %copy-start.42 = (bf16[1,32,16,512]{3,2,0,1:T(8,128)(2,1)}, bf16[1,32,16,512]{3,2,0,1:T(8,128)(2,1)S(1)}, u32[]{:S(2)}) copy-start(bf16[1,32,16,512]{3,2,0,1:T(8,128)(2,1)S(1)} %get-tuple-element.12) | copy-start | bytes 1572868
  391.7 1.8 copy-start.74
  392.1 1.8 copy-start.66
  392.4 1.9 copy-start.65
  392.8 1.9 copy-start.64
  393.2 1.9 copy-start.54
  393.5 1.9 copy-start.52
  393.9 1.8 copy-start.62
  394.3 1.8 copy-start.61
  394.6 1.8 copy-start.60
  395.0 1.8 copy-start.50
  395.4 1.8 copy-start.59
  395.7 1.8 copy-start.58
  396.1 1.8 copy-start.49
  396.4 1.8 copy-start.57
  396.8 1.9 copy-start.56
  397.2 1.8 copy-start.72
  397.5 1.8 copy-start.55
  397.9 1.8 copy-start.53
  398.3 1.8 copy-start.48
  398.6 1.8 copy-start.51
  403.3 31.6 %collective-permute-start.1 = (bf16[1,2,128,512]{3,2,1,0:T(8,128)(2,1)S(1)}, bf16[1,2,128,512]{3,2,1,0:T(8,128)(2,1)S(1)}, u32[]{:S(2)}, u32[]{:S(2)}) collective-permute-start(bf16[1,2,128,512]{3,2,1,0:T(8,128)(2,1)S(1)} %get-tuple-element.89), channel_id=1, source_target_pairs={{0,8},{8,16},{16,24},{24,32},{32,40},{40,48},{48,56},{56,64},{64,7... | collective-permute-start | bytes 786440 | tf_op jit(solution)/shard_map/ppermute | solution.py:13
  405.2 29.7 %collective-permute-start = (bf16[1,2,128,512]{3,2,1,0:T(8,128)(2,1)S(1)}, bf16[1,2,128,512]{3,2,1,0:T(8,128)(2,1)S(1)}, u32[]{:S(2)}, u32[]{:S(2)}) collective-permute-start(bf16[1,2,128,512]{3,2,1,0:T(8,128)(2,1)S(1)} %get-tuple-element.89), channel_id=1, source_target_pairs={{0,16},{8,24},{16,32},{24,40},{32,48},{40,56},{48,64},{56,72},{64,... | collective-permute-start | bytes 786440 | tf_op jit(solution)/shard_map/ppermute | solution.py:13
  433.4 7.9 %copy-start.41 = (bf16[1,32,16,512]{3,2,0,1:T(8,128)(2,1)S(1)}, bf16[1,32,16,512]{3,2,0,1:T(8,128)(2,1)}, u32[]{:S(2)}) copy-start(bf16[1,32,16,512]{3,2,0,1:T(8,128)(2,1)} %copy-done.40) | copy-start | bytes 1572868
  433.4 8.2 %copy-start.37 = (bf16[1,32,16,512]{3,2,0,1:T(8,128)(2,1)S(1)}, bf16[1,32,16,512]{3,2,0,1:T(8,128)(2,1)}, u32[]{:S(2)}) copy-start(bf16[1,32,16,512]{3,2,0,1:T(8,128)(2,1)} %copy-done.36) | copy-start | bytes 1572868
  435.0 18.6 %copy-start.39 = (bf16[1,32,16,512]{3,2,0,1:T(8,128)(2,1)S(1)}, bf16[1,32,16,512]{3,2,0,1:T(8,128)(2,1)}, u32[]{:S(2)}) copy-start(bf16[1,32,16,512]{3,2,0,1:T(8,128)(2,1)} %copy-done.38) | copy-start | bytes 1572868
  435.1 18.9 %copy-start.33 = (bf16[1,32,16,512]{3,2,0,1:T(8,128)(2,1)S(1)}, bf16[1,32,16,512]{3,2,0,1:T(8,128)(2,1)}, u32[]{:S(2)}) copy-start(bf16[1,32,16,512]{3,2,0,1:T(8,128)(2,1)} %copy-done.32) | copy-start | bytes 1572868
  435.1 19.5 %collective-permute-start.2 = (bf16[3,1,128,512]{3,2,1,0:T(8,128)(2,1)S(1)}, bf16[3,1,128,512]{3,2,1,0:T(8,128)(2,1)S(1)}, u32[]{:S(2)}, u32[]{:S(2)}) collective-permute-start(bf16[3,1,128,512]{3,2,1,0:T(8,128)(2,1)S(1)} %get-tuple-element.87), channel_id=1, source_target_pairs={{0,1},{1,2},{2,3},{3,4},{4,5},{5,6},{6,7},{8,9},{9,10},{10,11},{11... | collective-permute-start | bytes 1179656 | tf_op jit(solution)/shard_map/ppermute | solution.py:23
  439.2 14.4 %collective-permute-start.3 = (bf16[3,1,128,512]{3,2,1,0:T(8,128)(2,1)S(1)}, bf16[3,1,128,512]{3,2,1,0:T(8,128)(2,1)S(1)}, u32[]{:S(2)}, u32[]{:S(2)}) collective-permute-start(bf16[3,1,128,512]{3,2,1,0:T(8,128)(2,1)S(1)} %get-tuple-element.88), channel_id=1, source_target_pairs={{1,0},{2,1},{3,2},{4,3},{5,4},{6,5},{7,6},{9,8},{10,9},{11,10},{12... | collective-permute-start | bytes 1179656 | tf_op jit(solution)/shard_map/ppermute | solution.py:24
  441.3 13.0 %copy-start.35 = (bf16[1,32,16,512]{3,2,0,1:T(8,128)(2,1)S(1)}, bf16[1,32,16,512]{3,2,0,1:T(8,128)(2,1)}, u32[]{:S(2)}) copy-start(bf16[1,32,16,512]{3,2,0,1:T(8,128)(2,1)} %copy-done.34) | copy-start | bytes 1572868
  456.4 1.7 copy-start.17
  457.2 1.8 copy-start.5
  458.0 1.6 copy-start.19
  (21 other events, 27.0 us)
